TPU v7x, 32 devices: a whole 2x2x4 slice. The times are simulated.
32 devices in a mesh: blk: 4 (over z), rows: 8 (over y, x, core).
Axes of the slice: x: 2, y: 2, z: 4, core: 2. Of those that a mesh axis runs over, the one named last changes fastest.
Arguments:
- features: bfloat16 [4, 4096, 2048], P(None, ('blk', 'rows')), may hold values from -6 to 6
- owner_ids: int32 [4096, 1], P(('blk', 'rows')), may hold values from 0 to 7; in each aligned block of 128 rows (0 to 127, 128 to 255, ...) at most 32 rows name the same one
- test_blocks: bfloat16 [4, 192, 2048], P(None, 'blk'), may hold values from -0.0625 to 0.0625
Outputs:
- scores: bfloat16 [8192, 192], P(('blk', 'rows'))
Inputs may be any that keep to these rules, and one draw needn't show every extreme that they name: `owner_ids`: within each aligned block of 128 rows (the rows of one device) no owner is named more than 32 times.
All inputs are finite; a program needn't handle non-finite values.
Results may differ from a plain program's by a relative error of at most 0.001.
Values may be sent and summed in bfloat16 or wider, within the bound.
No kernel may reach another device: no remote copies, remote signals or barrier semaphores. Data moves between devices by JAX's collectives and lax.ppermute only.
A program may use at most 128 MiB of HBM per device.

v0:
```python
import jax
import jax.numpy as jnp
from jax import lax
from jax.sharding import PartitionSpec as P


def slot_matrix(owner_ids, owners_n, capacity):
    owner = owner_ids[:, 0]
    onehot = (owner[:, None] == jnp.arange(owners_n, dtype=jnp.int32)[None, :]).astype(jnp.int32)
    before = jnp.cumsum(onehot, axis=0) - onehot
    rank = jnp.sum(before * onehot, axis=1)
    slot = owner * capacity + rank
    slots = jnp.arange(owners_n * capacity, dtype=jnp.int32)
    return (slots[:, None] == slot[None, :]).astype(jnp.bfloat16)


def on_device(features, owner_ids, test_blocks):
    owners_n = lax.axis_size("rows")
    local_rows = features.shape[1]
    capacity = 2 * local_rows // owners_n
    tests = lax.all_gather(test_blocks, "blk", axis=1, tiled=True)
    total = jnp.einsum("rsk,rtk->st", features, tests, preferred_element_type=jnp.float32)
    row_scores = total.astype(jnp.bfloat16)
    placed = jnp.dot(
        slot_matrix(owner_ids, owners_n, capacity), row_scores, preferred_element_type=jnp.float32
    ).astype(jnp.bfloat16)
    return lax.all_to_all(placed, "rows", split_axis=0, concat_axis=0, tiled=True)


def solution(mesh):
    return jax.shard_map(
        on_device,
        mesh=mesh,
        in_specs=(P(None, ("blk", "rows"), None), P(("blk", "rows"), None), P(None, "blk", None)),
        out_specs=P(("blk", "rows"), None),
        check_vma=False,
    )
```

profile of v0, /device:TPU:0, one launch (start us, length us, event | category | flops | bytes accessed | tf_op | source)
XLA Modules:
  0.0 95.1 jit_solution(11568899653987399284)
XLA Ops:
  6.5 0.0 copy-start
  6.5 0.0 all-gather.2.cloned.1.call-start
  6.5 0.7 all-gather.2.cloned.1.call-update
  7.3 0.7 fusion.2
  8.0 0.2 reduce_window_sum.11
  8.2 0.8 select_reduce_fusion
  9.0 0.7 multiply_add_fusion
  9.7 65.4 %all-gather.2.cloned.1.call-done = bf16[4,192,2048]{2,1,0:T(8,128)(2,1)} async-done(((bf16[4,48,2048]{2,1,0:T(8,128)(2,1)}), bf16[4,192,2048]{2,1,0:T(8,128)(2,1)}) %all-gather.2.cloned.1.call-update) | async-done | bytes 3145744 | tf_op jit(solution)/shard_map/all_gather | solution.py:21
  75.1 0.0 copy-done
  75.1 3.4 %convolution_convert_fusion = bf16[256,192]{0,1:T(8,128)(2,1)S(1)} fusion(bf16[4,128,2048]{2,1,0:T(8,128)(2,1)S(1)} %copy-done, bf16[4,192,2048]{2,1,0:T(8,128)(2,1)} %all-gather.2.cloned.1.call-done, s32[128]{0:T(128)S(1)} %multiply_add_fusion), kind=kOutput, calls=%fused_computation | convolution fusion | flops 415342592 | bytes 5341696 | tf_op jit(solution)/shard_map/dot_general | solution.py:24
  78.5 0.1 copy.4
  78.6 8.9 %all_to_all.12 = bf16[8,32,192]{2,1,0:T(8,128)(2,1)S(1)} all-to-all(bf16[8,32,192]{2,1,0:T(8,128)(2,1)S(1)} %bitcast.12), channel_id=1, replica_groups=mesh['blk'=4,'rows'=8] {'rows'}, dimensions={0} | all-to-all | bytes 196608 | tf_op jit(solution)/shard_map/all_to_all | solution.py:27
  87.5 0.7 copy.5
Async XLA Ops:
  6.5 68.6 %copy-start = (bf16[4,128,2048]{2,1,0:T(8,128)(2,1)S(1)}, bf16[4,128,2048]{2,1,0:T(8,128)(2,1)}, u32[]{:S(2)}) copy-start(bf16[4,128,2048]{2,1,0:T(8,128)(2,1)} %param.3) | copy-start | bytes 6291460
  6.5 68.6 %all-gather.2.cloned.1.call-start = ((), (), s32[]{:S(2)}) async-start(), calls=%async_computation.1 | async-start | bytes 3932160 | tf_op jit(solution)/shard_map/all_gather | solution.py:21
Sparse Core Ops, SparseCore 0:
  8.9 66.1 all-gather.1
where the time goes:
time: 95.3 us; the launch traced here: 95.1 us
  waiting for transfers between devices  66.2 us (69%)
  between operations  13.4 us (14%)
  blocking collectives  8.93 us (9%)
  matrix products  3.37 us (4%)
  other arithmetic  2.4 us (3%)
    all_gather x1, waiting for transfers between devices, on_device(): tests = lax.all_gather(test_blocks, 'blk', axis=1, tiled=True)  65.4 us
    all_to_all x1, blocking collectives, on_device(): lax.all_to_all(placed, 'rows', split_axis=0, concat_axis=0, tiled=True)  8.93 us
    dot_general x1, matrix products, on_device(): jnp.dot(slot_matrix(owner_ids, owners_n, capacity), row_scores, preferred...  3.37 us
  transfers between devices with their start and end apart: 1, of which 1 were waited for; matrix products, arithmetic and copies ran while one was open for 3% of the time, Pallas kernels for 0%

commit v1 on v0

--- a/solution.py
+++ b/solution.py
@@ -18,7 +18,12 @@
     owners_n = lax.axis_size("rows")
     local_rows = features.shape[1]
     capacity = 2 * local_rows // owners_n
-    tests = lax.all_gather(test_blocks, "blk", axis=1, tiled=True)
+    ring = [test_blocks]
+    for hop in range(3):
+        ring.append(lax.ppermute(ring[-1], "blk", [(dev, (dev + 1) % 4) for dev in range(4)]))
+    tests = jnp.roll(
+        jnp.concatenate(ring[::-1], axis=1), (lax.axis_index("blk") + 1) * ring[0].shape[1], axis=1
+    )
     total = jnp.einsum("rsk,rtk->st", features, tests, preferred_element_type=jnp.float32)
     row_scores = total.astype(jnp.bfloat16)
     placed = jnp.dot(

time: 95.3 us -> 91.9 us (0.964)
  local copies, waits for them, and re-layouts: 0.85 us -> 16.3 us
  between operations: 13.4 us -> 0.05 us
  waiting for transfers between devices: 66.2 us -> 57.9 us
  starting transfers between devices: 0.01 us -> 3.03 us
    all_gather x1 -> x0, waiting for transfers between devices: 65.4 us -> none  [on_device(): tests = lax.all_gather(test_blocks, 'blk', axis=1, tiled=True)]
    ppermute x0 -> x3, waiting for transfers between devices: none -> 57.9 us  [on_device(): lax.ppermute(ring[-1], 'blk', [(dev, (dev + 1) % 4) for dev in range(4)])]
    unnamed x2 -> x15, local copies, waits for them, and re-layouts: 0.01 us -> 14.5 us
    ppermute x0 -> x3, starting transfers between devices: none -> 3.03 us  [on_device(): lax.ppermute(ring[-1], 'blk', [(dev, (dev + 1) % 4) for dev in range(4)])]
    concatenate x0 -> x1, local copies, waits for them, and re-layouts: none -> 0.99 us  [on_device(): jnp.roll(jnp.concatenate(ring[::-1], axis=1), (lax.axis_index('blk') + 1)...]
  transfers between devices with their start and end apart: 1 -> 3, of which waited for: 1 -> 3; matrix products, arithmetic and copies ran while one was open for 3% -> 3% of each run, Pallas kernels for 0% -> 0%
where the time goes in v1:
time: 91.9 us; the launch traced here: 91.4 us
  waiting for transfers between devices  57.9 us (63%)
  local copies, waits for them, and re-layouts  16.3 us (18%)
  blocking collectives  8.63 us (9%)
  matrix products  3.06 us (3%)
  starting transfers between devices  3.03 us (3%)
  other arithmetic  2.47 us (3%)
    ppermute x3, waiting for transfers between devices, on_device(): lax.ppermute(ring[-1], 'blk', [(dev, (dev + 1) % 4) for dev in range(4)])  57.9 us
    unnamed x15, local copies, waits for them, and re-layouts  14.5 us
    all_to_all x1, blocking collectives, on_device(): lax.all_to_all(placed, 'rows', split_axis=0, concat_axis=0, tiled=True)  8.63 us
    dot_general x1, matrix products, on_device(): jnp.dot(slot_matrix(owner_ids, owners_n, capacity), row_scores, preferred...  3.06 us
    ppermute x3, starting transfers between devices, on_device(): lax.ppermute(ring[-1], 'blk', [(dev, (dev + 1) % 4) for dev in range(4)])  3.03 us
  transfers between devices with their start and end apart: 3, of which 3 were waited for; matrix products, arithmetic and copies ran while one was open for 3% of the time, Pallas kernels for 0%

profile of v1, /device:TPU:0, one launch (start us, length us, event | category | flops | bytes accessed | tf_op | source)
XLA Modules:
  0.0 91.4 jit_solution(14133542217606283761)
XLA Ops:
  0.0 0.0 copy-start
  0.0 0.0 copy-start.1
  0.0 3.0 %collective-permute-start = (bf16[4,48,2048]{2,1,0:T(8,128)(2,1)}, bf16[4,48,2048]{2,1,0:T(8,128)(2,1)S(1)}, u32[]{:S(2)}, u32[]{:S(2)}) collective-permute-start(bf16[4,48,2048]{2,1,0:T(8,128)(2,1)} %param.5), channel_id=1, source_target_pairs={{0,8},{8,16},{16,24},{24,0},{1,9},{9,17},{17,25},{25,1},{2,10},{10... | collective-permute-start | bytes 2359304 | tf_op jit(solution)/shard_map/ppermute | solution.py:23
  3.0 19.8 %collective-permute-done = bf16[4,48,2048]{2,1,0:T(8,128)(2,1)S(1)} collective-permute-done((bf16[4,48,2048]{2,1,0:T(8,128)(2,1)}, bf16[4,48,2048]{2,1,0:T(8,128)(2,1)S(1)}, u32[]{:S(2)}, u32[]{:S(2)}) %collective-permute-start) | collective-permute-done | bytes 786464 | tf_op jit(solution)/shard_map/ppermute | solution.py:23
  22.8 0.0 copy-start.2
  22.8 0.9 copy-done.2
  23.7 0.0 collective-permute-start.1
  23.7 20.6 %collective-permute-done.1 = bf16[4,48,2048]{2,1,0:T(8,128)(2,1)} collective-permute-done((bf16[4,48,2048]{2,1,0:T(8,128)(2,1)S(1)}, bf16[4,48,2048]{2,1,0:T(8,128)(2,1)}, u32[]{:S(2)}, u32[]{:S(2)}) %collective-permute-start.1) | collective-permute-done | bytes 786464 | tf_op jit(solution)/shard_map/ppermute | solution.py:23
  44.3 0.0 collective-permute-start.2
  44.4 0.7 fusion.11
  45.1 0.2 reduce_window_sum.11
  45.3 0.0 copy-start.3
  45.3 0.9 select_reduce_fusion
  46.2 0.7 multiply_add_fusion
  46.8 17.4 %collective-permute-done.2 = bf16[4,48,2048]{2,1,0:T(8,128)(2,1)} collective-permute-done((bf16[4,48,2048]{2,1,0:T(8,128)(2,1)}, bf16[4,48,2048]{2,1,0:T(8,128)(2,1)}, u32[]{:S(2)}, u32[]{:S(2)}) %collective-permute-start.2) | collective-permute-done | bytes 786464 | tf_op jit(solution)/shard_map/ppermute | solution.py:23
  64.3 2.1 %constant_dynamic-update-slice_fusion.7 = bf16[4,384,2048]{2,1,0:T(8,128)(2,1)} fusion(bf16[4,48,2048]{2,1,0:T(8,128)(2,1)} %collective-permute-done.2), kind=kLoop, calls=%fused_computation.17 | loop fusion | bytes 1572864
  66.4 2.1 %constant_dynamic-update-slice_fusion.6 = bf16[4,384,2048]{2,1,0:T(8,128)(2,1)} fusion(bf16[4,384,2048]{2,1,0:T(8,128)(2,1)} %constant_dynamic-update-slice_fusion.7, bf16[4,48,2048]{2,1,0:T(8,128)(2,1)} %collective-permute-done.1), kind=kLoop, calls=%fused_computation.16 | loop fusion | bytes 1572864
  68.5 2.1 %constant_dynamic-update-slice_fusion.5 = bf16[4,384,2048]{2,1,0:T(8,128)(2,1)} fusion(bf16[4,384,2048]{2,1,0:T(8,128)(2,1)} %constant_dynamic-update-slice_fusion.6, bf16[4,48,2048]{2,1,0:T(8,128)(2,1)} %copy-done.2), kind=kLoop, calls=%fused_computation.15 | loop fusion | bytes 1572864
  70.6 2.1 %constant_dynamic-update-slice_fusion.4 = bf16[4,384,2048]{2,1,0:T(8,128)(2,1)} fusion(bf16[4,384,2048]{2,1,0:T(8,128)(2,1)} %constant_dynamic-update-slice_fusion.5, bf16[4,48,2048]{2,1,0:T(8,128)(2,1)} %param.5), kind=kLoop, calls=%fused_computation.14 | loop fusion | bytes 1572864
  72.7 2.1 %constant_dynamic-update-slice_fusion.3 = bf16[4,384,2048]{2,1,0:T(8,128)(2,1)} fusion(bf16[4,384,2048]{2,1,0:T(8,128)(2,1)} %constant_dynamic-update-slice_fusion.4, bf16[4,48,2048]{2,1,0:T(8,128)(2,1)} %collective-permute-done.2), kind=kLoop, calls=%fused_computation.13 | loop fusion | bytes 1572864
  74.8 2.1 %constant_dynamic-update-slice_fusion.2 = bf16[4,384,2048]{2,1,0:T(8,128)(2,1)} fusion(bf16[4,384,2048]{2,1,0:T(8,128)(2,1)} %constant_dynamic-update-slice_fusion.3, bf16[4,48,2048]{2,1,0:T(8,128)(2,1)} %collective-permute-done.1), kind=kLoop, calls=%fused_computation.12 | loop fusion | bytes 1572864
  76.9 0.0 copy-done.3
  76.9 0.9 %constant_dynamic-update-slice_fusion.1 = bf16[4,384,2048]{2,1,0:T(8,128)(2,1)} fusion(bf16[4,384,2048]{2,1,0:T(8,128)(2,1)} %constant_dynamic-update-slice_fusion.2, bf16[4,48,2048]{2,1,0:T(8,128)(2,1)S(1)} %copy-done.3), kind=kLoop, calls=%fused_computation.11 | loop fusion | bytes 1572864
  77.9 0.0 copy-done.1
  77.9 1.0 %constant_dynamic-update-slice_fusion = bf16[4,384,2048]{2,1,0:T(8,128)(2,1)} fusion(bf16[4,384,2048]{2,1,0:T(8,128)(2,1)} %constant_dynamic-update-slice_fusion.1, bf16[4,48,2048]{2,1,0:T(8,128)(2,1)S(1)} %copy-done.1), kind=kLoop, calls=%fused_computation.10 | loop fusion | bytes 1572864 | tf_op jit(solution)/shard_map/jit(_roll_dynamic)/concatenate | solution.py:24
  78.8 0.0 copy-done
  78.8 3.1 %convolution_convert_fusion = bf16[256,192]{0,1:T(8,128)(2,1)S(1)} fusion(bf16[4,128,2048]{2,1,0:T(8,128)(2,1)S(1)} %copy-done, bf16[4,384,2048]{2,1,0:T(8,128)(2,1)} %constant_dynamic-update-slice_fusion, s32[]{:T(128)S(6)} %select_n.14, s32[128]{0:T(128)S(1)} %multiply_add_fusion), kind=kOutput, calls=%fused_computation.2 | convolution fusion | flops 415342592 | bytes 5341700 | tf_op jit(solution)/shard_map/dot_general | solution.py:29
  81.9 0.1 copy.4
  82.0 8.6 %all_to_all.12 = bf16[8,32,192]{2,1,0:T(8,128)(2,1)S(1)} all-to-all(bf16[8,32,192]{2,1,0:T(8,128)(2,1)S(1)} %bitcast.11), channel_id=1, replica_groups=mesh['blk'=4,'rows'=8] {'rows'}, dimensions={0} | all-to-all | bytes 196608 | tf_op jit(solution)/shard_map/all_to_all | solution.py:32
  90.6 0.7 copy.5
Async XLA Ops:
  0.0 78.8 %copy-start = (bf16[4,128,2048]{2,1,0:T(8,128)(2,1)S(1)}, bf16[4,128,2048]{2,1,0:T(8,128)(2,1)}, u32[]{:S(2)}) copy-start(bf16[4,128,2048]{2,1,0:T(8,128)(2,1)} %param.3) | copy-start | bytes 6291460
  0.0 77.9 %copy-start.1 = (bf16[4,48,2048]{2,1,0:T(8,128)(2,1)S(1)}, bf16[4,48,2048]{2,1,0:T(8,128)(2,1)}, u32[]{:S(2)}) copy-start(bf16[4,48,2048]{2,1,0:T(8,128)(2,1)} %param.5) | copy-start | bytes 2359300
  0.0 22.8 %collective-permute-start = (bf16[4,48,2048]{2,1,0:T(8,128)(2,1)}, bf16[4,48,2048]{2,1,0:T(8,128)(2,1)S(1)}, u32[]{:S(2)}, u32[]{:S(2)}) collective-permute-start(bf16[4,48,2048]{2,1,0:T(8,128)(2,1)} %param.5), channel_id=1, source_target_pairs={{0,8},{8,16},{16,24},{24,0},{1,9},{9,17},{17,25},{25,1},{2,10},{10... | collective-permute-start | bytes 2359304 | tf_op jit(solution)/shard_map/ppermute | solution.py:23
  22.8 0.9 copy-start.2
  23.7 20.6 %collective-permute-start.1 = (bf16[4,48,2048]{2,1,0:T(8,128)(2,1)S(1)}, bf16[4,48,2048]{2,1,0:T(8,128)(2,1)}, u32[]{:S(2)}, u32[]{:S(2)}) collective-permute-start(bf16[4,48,2048]{2,1,0:T(8,128)(2,1)S(1)} %collective-permute-done), channel_id=1, source_target_pairs={{0,8},{8,16},{16,24},{24,0},{1,9},{9,17},{17,25},{25,1},{2,10},{10... | collective-permute-start | bytes 2359304 | tf_op jit(solution)/shard_map/ppermute | solution.py:23
  44.3 19.9 %collective-permute-start.2 = (bf16[4,48,2048]{2,1,0:T(8,128)(2,1)}, bf16[4,48,2048]{2,1,0:T(8,128)(2,1)}, u32[]{:S(2)}, u32[]{:S(2)}) collective-permute-start(bf16[4,48,2048]{2,1,0:T(8,128)(2,1)} %collective-permute-done.1), channel_id=1, source_target_pairs={{0,8},{8,16},{16,24},{24,0},{1,9},{9,17},{17,25},{25,1},{2,10},{10... | collective-permute-start | bytes 2359304 | tf_op jit(solution)/shard_map/ppermute | solution.py:23
  45.3 31.6 %copy-start.3 = (bf16[4,48,2048]{2,1,0:T(8,128)(2,1)S(1)}, bf16[4,48,2048]{2,1,0:T(8,128)(2,1)}, u32[]{:S(2)}) copy-start(bf16[4,48,2048]{2,1,0:T(8,128)(2,1)} %copy-done.2) | copy-start | bytes 2359300
